TPU v7x, 256 devices: a whole 4x4x8 slice. The times are simulated.
256 devices in a mesh: wall: 8 (over y_lo, x), stream: 32 (over z, y_hi, core).
Axes of the slice: x: 4, y: 4 (y_hi: 2, y_lo: 2; y = y_hi * 2 + y_lo), z: 8, core: 2. Of those that a mesh axis runs over, the one named last changes fastest.
Arguments:
- velocity: float32 [3, 64, 512, 128], P(None, 'wall', 'stream'), may hold values from -6 to 6
- sample_block: int32 [8, 256], P('wall', 'stream'), may hold values from 0 to 127
- sample_member: int32 [8, 256, 1], P('wall', 'stream'), may hold values from 0 to 7; in each aligned block of 8 rows (0 to 7, 8 to 15, ..., all dimensions but the last counted through in order) at most 2 rows name the same one
- k_first: bfloat16 [8, 54, 64], P('wall'), may hold values from -6 to 6
- k_second: bfloat16 [8, 27, 64, 64], P('wall'), may hold values from -6 to 6
- w_hidden: bfloat16 [8, 2048, 2048], P('wall'), may hold values from -6 to 6
- w_out: bfloat16 [8, 2048, 2], P('wall'), may hold values from -6 to 6
Outputs:
- new_field: float32 [3, 64, 512, 128], P(None, 'wall', 'stream')
- stress: float32 [2, 8, 256], P(None, 'wall', 'stream')
- new_k_first: float32 [8, 54, 64], P('wall')
- new_k_second: float32 [8, 27, 64, 64], P('wall')
- new_w_hidden: float32 [8, 2048, 2048], P('wall', 'stream')
- new_w_out: float32 [8, 2048, 2], P('wall')
Inputs may be any that keep to these rules, and one draw needn't show every extreme that they name: `sample_member`: in the list of one slab at most 2 samples name the same member; in every draw some slab names some member exactly 2 times.
All inputs are finite; a program needn't handle non-finite values.
Results may differ from a plain program's by a relative error of at most 0.0064.
Values may be sent and summed in bfloat16 or wider, within the bound.
No kernel may reach another device: no remote copies, remote signals or barrier semaphores. Data moves between devices by JAX's collectives and lax.ppermute only.
A program may use at most 128 MiB of HBM per device.

v0:
```python
import math
import jax
import jax.numpy as jnp
import numpy as np
from jax import lax
from jax.sharding import Mesh
from jax.sharding import PartitionSpec as P

P_SIZE = 8
PY = 4
PX = 4
PZ = 8
CH = 64
CAP = 2
FEATS = 2048
STREAM = ("stream_0", "stream_1", "stream_2")
highest = lax.Precision.HIGHEST
time_step = 0.005
relax_rate = 20.0
viscosity = 0.3
learn_rate = 0.5
rms_eps = 1e-06


def extended(shard, sides, width):
    edges = {}
    for axis, dim in sides:
        size, length = (lax.axis_size(axis), shard.shape[dim])
        up = [(i, (i + 1) % size) for i in range(size)]
        last = lax.slice_in_dim(shard, length - width, length, axis=dim)
        first = lax.slice_in_dim(shard, 0, width, axis=dim)
        edges[dim] = (
            lax.ppermute(last, axis, up),
            lax.ppermute(first, axis, [(b, a) for a, b in up]),
        )
    done = []
    for _, dim in sides:
        low, high = edges[dim]
        around = [(width, width) if d in done else (0, 0) for d in range(shard.ndim)]
        shard = jnp.concatenate([jnp.pad(low, around), shard, jnp.pad(high, around)], axis=dim)
        done.append(dim)
    return shard


def in_one_piece(arrays, axis, split_dim, concat_dim, along):
    widths = [math.prod(a.shape[along:]) for a in arrays]
    both = jnp.concatenate(
        [a.reshape(*a.shape[:along], w) for a, w in zip(arrays, widths)], axis=along
    )
    whole = lax.all_to_all(both, axis, split_axis=split_dim, concat_axis=concat_dim, tiled=True)
    tiles = jnp.split(whole, [sum(widths[:k]) for k in range(1, len(widths))], axis=along)
    return tuple((b.reshape(*whole.shape[:along], *a.shape[along:]) for a, b in zip(arrays, tiles)))


def joined_along(tiles, dim):
    lengths = list(tiles.shape[1:])
    lengths[dim] *= tiles.shape[0]
    return jnp.moveaxis(tiles, 0, dim).reshape(lengths)


def gather_in_order(shard, axes, order):
    tiles = shard
    for k in order:
        tiles = lax.all_gather(tiles, axes[k])
    done = order[::-1]
    back = [done.index(k) for k in range(len(axes))]
    tiles = tiles.transpose(*back, *range(len(axes), tiles.ndim))
    return tiles.reshape(-1, *shard.shape)


def gathered_by_axis(shard, axes, order, dim):
    return joined_along(gather_in_order(shard, axes, order), dim)


def cheb_tables(points):
    order = points - 1
    node_index = np.arange(points)
    nodes = -np.cos(np.pi * node_index / order)
    end_weight = np.where((node_index == 0) | (node_index == order), 2.0, 1.0)
    parity = (-1.0) ** (node_index[:, None] + node_index[None, :])
    offdiag = 1.0 - np.eye(points)
    spread = nodes[:, None] - nodes[None, :] + np.eye(points)
    deriv = end_weight[:, None] / end_weight[None, :] * parity / spread * offdiag
    deriv = deriv - np.eye(points) * deriv.sum(axis=1)[:, None]
    highpass = parity / (order * end_weight[None, :])
    return (deriv, highpass, 0.5 * order * order)


def axis_matrices(count, periodic):
    deriv, highpass, lift_half = cheb_tables(P_SIZE)
    length = count * P_SIZE
    slope = np.kron(np.eye(count), deriv)
    upper = np.kron(np.eye(count), highpass)
    faces = count if periodic else count - 1
    for element in range(faces):
        last_node = element * P_SIZE + P_SIZE - 1
        next_node = (element + 1) % count * P_SIZE
        slope[last_node, next_node] += lift_half
        slope[last_node, last_node] -= lift_half
        slope[next_node, last_node] -= lift_half
        slope[next_node, next_node] += lift_half
    if not periodic:
        slope[0, 0] += lift_half
        slope[length - 1, length - 1] -= lift_half
    paired = jnp.asarray(np.concatenate([slope, upper], axis=0), jnp.float32)
    return (paired, lift_half)


def slot_matrix(members, member_count):
    member_hot = (members[..., None] == jnp.arange(member_count, dtype=jnp.int32)).astype(jnp.int32)
    before = jnp.cumsum(member_hot, axis=-2) - member_hot
    ranks = jnp.sum(before * member_hot, axis=-1)
    slots = members * CAP + ranks
    return (slots[..., None, :] == jnp.arange(member_count * CAP, dtype=jnp.int32)[:, None]).astype(
        jnp.float32
    )


DIMS = ("NDHWC", "DHWIO", "NDHWC")
FILTER_DIMS = ("CDHWN", "IDHWO", "NDHWC")
SAME = ((1, 1), (1, 1), (1, 1))


def silu_slope(value):
    gate = jax.nn.sigmoid(value)
    return gate * (1.0 + value * (1.0 - gate))


def conv_taps(grid, kernel):
    return lax.conv_general_dilated(
        grid, kernel, (1, 1, 1), SAME, dimension_numbers=DIMS, preferred_element_type=jnp.float32
    )


def conv_filter(grid, delta):
    taps = lax.conv_general_dilated(
        grid,
        delta,
        (1, 1, 1),
        SAME,
        dimension_numbers=FILTER_DIMS,
        preferred_element_type=jnp.float32,
    )
    return jnp.moveaxis(taps, 0, 3)


def forward_back(patches, aim_rows, valid, k_first, k_second, w_hidden, w_out):
    batch = patches.shape[0]
    channels = k_second.shape[-1]
    inputs = patches.reshape(batch, 2, PY, PX, PZ).transpose(0, 2, 3, 4, 1)
    first_taps = k_first.reshape(3, 3, 3, 2, channels)
    second_taps = k_second.reshape(3, 3, 3, channels, channels)
    scale_one = 1.0 / math.sqrt(54.0)
    scale_two = 1.0 / math.sqrt(27.0 * channels)
    scale_three = 1.0 / math.sqrt(1.0 * w_hidden.shape[0])
    scale_four = 1.0 / math.sqrt(1.0 * w_hidden.shape[1])
    pre_one = conv_taps(inputs, first_taps) * scale_one
    hidden_one = jax.nn.silu(pre_one).astype(jnp.bfloat16)
    pre_two = conv_taps(hidden_one, second_taps) * scale_two
    pooled = (
        jax.nn.silu(pre_two).reshape(batch, PY // 2, 2, PX // 2, 2, PZ, channels).mean(axis=(2, 4))
    )
    features = pooled.reshape(batch, -1).astype(jnp.bfloat16)
    pre_three = jnp.dot(features, w_hidden, preferred_element_type=jnp.float32) * scale_three
    hidden_three = jax.nn.silu(pre_three).astype(jnp.bfloat16)
    pred = jnp.dot(hidden_three, w_out, preferred_element_type=jnp.float32) * scale_four
    error = valid.astype(jnp.float32)[:, None] * (pred - aim_rows.astype(jnp.float32))
    grad_out = jnp.dot(hidden_three.astype(jnp.float32).T, error, precision=highest) * scale_four
    delta_three = (
        jnp.dot(error, w_out.astype(jnp.float32).T, precision=highest)
        * scale_four
        * silu_slope(pre_three)
    ).astype(jnp.bfloat16)
    back_feat = jnp.dot(delta_three, w_hidden.T, preferred_element_type=jnp.float32) * scale_three
    back_grid = back_feat.reshape(batch, PY // 2, 1, PX // 2, 1, PZ, channels)
    spread_back = (
        jnp.broadcast_to(back_grid, (batch, PY // 2, 2, PX // 2, 2, PZ, channels)).reshape(
            pre_two.shape
        )
        * 0.25
    )
    delta_two = (spread_back * silu_slope(pre_two)).astype(jnp.bfloat16)
    grad_two = (conv_filter(hidden_one, delta_two) * scale_two).reshape(27, channels, channels)
    mirrored = jnp.flip(second_taps, axis=(0, 1, 2)).swapaxes(3, 4)
    back_one = conv_taps(delta_two, mirrored)
    delta_one = (back_one * scale_two * silu_slope(pre_one)).astype(jnp.bfloat16)
    grad_one = (conv_filter(inputs, delta_one) * scale_one).reshape(54, channels)
    return (pred, grad_one, grad_two, grad_out, features, delta_three)


def row_update(weight, grad):
    scale = jnp.sqrt(jnp.mean(grad * grad, axis=-1, keepdims=True) + rms_eps)
    return weight.astype(jnp.float32) - learn_rate * grad / scale


def whole_update(weight, grad):
    scale = jnp.sqrt(jnp.mean(grad * grad) + rms_eps)
    return weight.astype(jnp.float32) - learn_rate * grad / scale


def body(velocity, sample_block, sample_member, k_first, k_second, w_hidden, w_out):
    wall_count = lax.axis_size("wall")
    wall_place = lax.axis_index("wall")
    flow_count = lax.axis_size(STREAM)
    flow_place = lax.axis_index(STREAM)
    padded = extended(velocity, (("wall", 1), (STREAM, 2)), 1)
    keep_low = (wall_place > 0).astype(jnp.float32)
    keep_high = (wall_place < wall_count - 1).astype(jnp.float32)
    below = padded[:, 0, 1:-1, :] * keep_low
    above = padded[:, -1, 1:-1, :] * keep_high
    left_face = padded[:, 1:-1, 0, :]
    right_face = padded[:, 1:-1, -1, :]
    size_y, size_x, size_z = (velocity.shape[1], velocity.shape[2], velocity.shape[3])
    pair_y, lift_half = axis_matrices(size_y // P_SIZE, False)
    pair_x, lift_same = axis_matrices(size_x // P_SIZE, False)
    pair_z, lift_again = axis_matrices(size_z // P_SIZE, True)
    along_y = jnp.einsum("cyxz,wy->cwxz", velocity, pair_y, precision=highest)
    grad_y = (
        along_y[:, :size_y]
        .at[:, 0]
        .add(-lift_half * below)
        .at[:, size_y - 1]
        .add(lift_half * above)
    )
    high_y = along_y[:, size_y:]
    along_x = jnp.einsum("cyxz,wx->cywz", velocity, pair_x, precision=highest)
    grad_x = (
        along_x[:, :, :size_x]
        .at[:, :, 0]
        .add(-lift_half * left_face)
        .at[:, :, size_x - 1]
        .add(lift_half * right_face)
    )
    high_x = along_x[:, :, size_x:]
    along_z = jnp.einsum("cyxz,wz->cyxw", velocity, pair_z, precision=highest)
    grad_z = along_z[..., :size_z]
    high_z = along_z[..., size_z:]
    advect = velocity[0][None] * grad_x + velocity[1][None] * grad_y + velocity[2][None] * grad_z
    new_field = velocity + time_step * (-advect - relax_rate * (high_x + high_y + high_z))
    rows_y, rows_x, rows_z = (size_y // PY, size_x // PX, size_z // PZ)
    tangent = jnp.stack([velocity[0], velocity[2]]).reshape(2, rows_y, PY, rows_x, PX, rows_z, PZ)
    blocks = tangent.transpose(1, 3, 5, 0, 2, 4, 6).reshape(-1, 2 * PY * PX * PZ)
    slope_wall = jnp.stack([grad_y[0], grad_y[2]]).reshape(2, rows_y, PY, rows_x, PX, rows_z, PZ)
    stress_true = (
        (viscosity * jnp.mean(slope_wall, axis=(2, 4, 6))).transpose(1, 2, 3, 0).reshape(-1, 2)
    )
    picked = sample_block.reshape(-1)
    members = sample_member.reshape(-1)
    patch_rows = jnp.take(blocks, picked, axis=0).astype(jnp.bfloat16)
    aim_rows = jnp.take(stress_true, picked, axis=0).astype(jnp.bfloat16)
    select = slot_matrix(members, wall_count)
    select_half = select.astype(jnp.bfloat16)
    send_rows = jnp.dot(select_half, patch_rows, preferred_element_type=jnp.float32).astype(
        jnp.bfloat16
    )
    send_aims = jnp.dot(select_half, aim_rows, preferred_element_type=jnp.float32).astype(
        jnp.bfloat16
    )
    send_valid = jnp.sum(select, axis=1).astype(jnp.bfloat16)
    recv_rows, recv_aims, recv_valid = in_one_piece(
        (send_rows, send_aims, send_valid), "wall", 0, 0, 1
    )
    pred, grad_one, grad_two, grad_out, features, delta_three = forward_back(
        recv_rows, recv_aims, recv_valid, k_first[0], k_second[0], w_hidden[0], w_out[0]
    )
    back = lax.all_to_all(pred, "wall", split_axis=0, concat_axis=0, tiled=True)
    stress_local = jnp.dot(select.T, back, precision=highest)
    stress = stress_local.T[:, None, :]
    share_rows = FEATS // flow_count
    dense_scale = 1.0 / math.sqrt(1.0 * FEATS)
    columns_here = lax.all_to_all(features, STREAM, split_axis=1, concat_axis=0, tiled=True)
    grad_hidden = (
        jnp.dot(
            columns_here.T,
            gathered_by_axis(delta_three, STREAM, (1, 0, 2), 0),
            preferred_element_type=jnp.float32,
        )
        * dense_scale
    )
    own_rows = lax.dynamic_slice_in_dim(w_hidden[0], flow_place * share_rows, share_rows, 0)
    new_w_hidden = row_update(own_rows, grad_hidden)[None]
    grad_one, grad_two, grad_out = lax.psum((grad_one, grad_two, grad_out), STREAM)
    new_k_second = row_update(k_second[0], grad_two)
    new_k_first = row_update(k_first[0], grad_one)
    new_w_out = whole_update(w_out[0], grad_out)
    return (new_field, stress, new_k_first[None], new_k_second[None], new_w_hidden, new_w_out[None])


def solution(mesh):
    torus = Mesh(
        mesh.devices.reshape(mesh.shape["wall"], 8, 2, 2),
        ("wall", "stream_0", "stream_1", "stream_2"),
    )
    in_specs = (
        P(None, "wall", STREAM, None),
        P("wall", STREAM),
        P("wall", STREAM, None),
        P("wall", None, None),
        P("wall", None, None, None),
        P("wall", None, None),
        P("wall", None, None),
    )
    out_specs = (
        P(None, "wall", STREAM, None),
        P(None, "wall", STREAM),
        P("wall", None, None),
        P("wall", None, None, None),
        P("wall", STREAM, None),
        P("wall", None, None),
    )
    return jax.shard_map(body, mesh=torus, in_specs=in_specs, out_specs=out_specs, check_vma=False)
```

profile of v0, /device:TPU:1, one launch (start us, length us, event | category | flops | bytes accessed | tf_op | source)
XLA Modules:
  0.0 358.8 jit_solution(1956748719228689826)
XLA Ops:
  8.0 0.8 fusion.47
  8.8 2.0 collective-permute-start.2
  10.9 2.4 collective-permute-start.3
  13.2 1.6 fusion.46
  14.8 4.0 %collective-permute-start = (f32[3,8,1,128]{3,2,1,0:T(1,128)}, f32[3,8,1,128]{3,2,1,0:T(1,128)}, u32[]{:S(2)}, u32[]{:S(2)}) collective-permute-start(f32[3,8,1,128]{3,2,1,0:T(1,128)} %get-tuple-element.94), channel_id=1, source_target_pairs={{0,1},{1,2},{2,3},{3,4},{4,5},{5,6},{6,7},{7,8},{8,9},{9,10},{10,1... | collective-permute-start | bytes 36872 | tf_op jit(solution)/shard_map/ppermute | solution.py:33
  18.8 0.7 fusion.41
  19.5 0.7 compare_and_fusion
  20.1 0.9 fusion.44
  21.0 1.5 convolution_bitcast_fusion
  22.5 1.5 fusion.23
  24.0 1.5 convolution_bitcast_fusion.1
  25.4 0.7 fusion.34
  26.2 0.8 select_reduce_fusion
  27.0 0.7 multiply_add_fusion
  27.7 1.2 reshape.297
  31.3 0.6 copy-done.1
  31.9 0.7 pad_maximum_fusion.1
  32.6 2.1 reshape.300
  35.6 0.9 convolution_convert_fusion.1
  36.6 0.7 pad_maximum_fusion.2
  37.3 3.3 all-to-all-start
  41.0 4.7 %all-to-all-done = bf16[8,2,259]{2,1,0:T(2,128)(2,1)S(1)} async-done(((bf16[8,2,259]{2,1,0:T(2,128)(2,1)}), bf16[8,2,259]{2,1,0:T(2,128)(2,1)S(1)}, u32[]{:S(2)}, u32[]{:S(2)}) %all-to-all-start) | async-done | bytes 8320 | tf_op jit(solution)/shard_map/all_to_all | solution.py:50
  46.0 0.9 convolution_multiply_fusion.4
  46.9 4.5 %fusion.14 = (f32[16,4,4,8,64]{4,0,3,2,1:T(8,128)}, f32[16,4,4,8,64]{4,0,3,2,1:T(8,128)}) fusion(bf16[3,3,3,64,64]{4,3,2,1,0:T(8,128)(2,1)} %bitcast.138, f32[16,4,4,8,64]{4,0,3,2,1:T(8,128)S(1)} %convolution_multiply_fusion.4), kind=kOutput, calls=%fused_computation.26 | convolution fusion | flops 289669120 | bytes 1794048 | tf_op jit(solution)/shard_map/conv_general_dilated | solution.py:130
  51.4 1.3 reduce_sum.75
  53.1 4.6 %multiply_convert_fusion.3 = (bf16[16,2048]{1,0:T(8,128)(2,1)S(1)}, f32[16,2048]{1,0:T(8,128)S(1)}) fusion(bf16[16,2048]{1,0:T(8,128)(2,1)S(1)} %convert_element_type.116, bf16[1,2048,2048]{2,1,0:T(8,128)(2,1)} %param.23), kind=kOutput, calls=%fused_computation.50 | convolution fusion | flops 134414336 | bytes 8650752 | tf_op jit(solution)/shard_map/dot_general | solution.py:164
  58.6 5.4 %all-gather = bf16[32,2048]{1,0:T(8,128)(2,1)} all-gather(bf16[16,2048]{1,0:T(8,128)(2,1)S(1)} %fusion.11), channel_id=2, replica_groups=mesh['wall'=8,'stream_0'=8,'stream_1'=2,'stream_2'=2] {'stream_1'}, dimensions={0}, use_global_device_ids=true | all-gather | bytes 196608 | tf_op jit(solution)/shard_map/all_gather | solution.py:64
  64.1 0.7 slice_add_fusion.5
  64.9 0.7 slice_add_fusion.4
  65.8 0.8 fusion.20
  66.6 5.7 %fusion.8 = f32[16,2048]{1,0:T(8,128)S(1)} fusion(bf16[16,2048]{1,0:T(8,128)(2,1)S(1)} %fusion.11, bf16[1,2048,2048]{2,1,0:T(8,128)(2,1)} %param.23), kind=kOutput, calls=%fused_computation.9 | convolution fusion | flops 134250496 | bytes 8585216 | tf_op jit(solution)/shard_map/dot_general | solution.py:174
  73.1 3.6 %convolution_multiply_fusion.5 = f32[3,3,3,64,64]{4,3,2,1,0:T(8,128)} fusion(bf16[16,4,4,8,64]{4,0,3,2,1:T(8,128)(2,1)S(1)} %multiply_convert_fusion, f32[16,4,4,8,64]{4,0,3,2,1:T(8,128)S(1)} %convolution_multiply_fusion.4), kind=kOutput, calls=%fused_computation.16 | convolution fusion | flops 289124352 | bytes 1228800 | tf_op jit(solution)/shard_map/transpose | solution.py:144
  77.1 4.2 %convolution_multiply_fusion.6 = f32[3,3,3,2,64]{4,3,2,1,0:T(2,128)S(1)} fusion(bf16[16,2,4,4,8]{0,4,3,2,1:T(8,128)(2,1)S(1)} %bitcast.141, bf16[16,4,4,8,64]{4,0,3,2,1:T(8,128)(2,1)S(1)} %multiply_convert_fusion, bf16[3,3,3,64,64]{4,3,2,1,0:T(8,128)(2,1)S(1)} %bitcast.139, f32[16,4,4,8,64]{4,0,3,2,1:T(8,128)S(1)} %convolution_multiply_fusion.4), kind=kOutput, calls=%fused_computation.20 | convolution fusion | flops 298683776 | bytes 1029632 | tf_op jit(solution)/shard_map/transpose | solution.py:144
  81.3 19.8 %all-gather.6.cloned.1.call-done = bf16[16,16,2048]{2,1,0:T(8,128)(2,1)} async-done(((bf16[2,16,2048]{2,1,0:T(8,128)(2,1)}), bf16[16,16,2048]{2,1,0:T(8,128)(2,1)}) %all-gather.6.cloned.1.call-update) | async-done | bytes 1048592 | tf_op jit(solution)/shard_map/all_gather | solution.py:64
  102.0 4.9 %all-to-all-start.1 = ((f32[8,2,2]{1,2,0:T(2,128)}), f32[8,2,2]{1,2,0:T(2,128)S(1)}, u32[]{:S(2)}, u32[]{:S(2)}) async-start(f32[8,2,2]{1,2,0:T(2,128)} %copy.77), calls=%async_computation.1 | async-start | bytes 16384 | tf_op jit(solution)/shard_map/all_to_all | solution.py:266
  107.0 128.6 %all-reduce = (f32[54,64]{1,0:T(8,128)S(1)}, f32[2048,2]{0,1:T(2,128)S(1)}) all-reduce(f32[54,64]{1,0:T(8,128)S(1)} %reshape.304, f32[2048,2]{0,1:T(2,128)S(1)} %convolution_multiply_fusion.1), channel_id=1, replica_groups=mesh['wall'=8,'stream_0'=8,'stream_1'=2,'stream_2'=2] {'stream_0','strea..., use_global_device_ids=true, to_apply=%region_5.6 | all-reduce | flops 7552 | bytes 60416 | tf_op jit(solution)/shard_map/psum | solution.py:282
  235.8 0.6 broadcast_in_dim.48
  236.4 0.6 multiply_reduce_fusion.3
  237.7 0.6 fusion.29
  238.4 0.8 reshape.333
  239.1 10.2 %all-to-all-start.2 = ((bf16[32,2,512]{2,1,0:T(2,128)(2,1)}), bf16[32,2,512]{2,1,0:T(2,128)(2,1)S(1)}, u32[]{:S(2)}, u32[]{:S(2)}) async-start(bf16[32,2,512]{2,1,0:T(2,128)(2,1)} %reshape.333), calls=%async_computation.2 | async-start | bytes 131072 | tf_op jit(solution)/shard_map/all_to_all | solution.py:271
  249.4 0.8 fusion.33
  250.2 9.0 %all-to-all-done.2 = bf16[32,2,512]{2,1,0:T(2,128)(2,1)S(1)} async-done(((bf16[32,2,512]{2,1,0:T(2,128)(2,1)}), bf16[32,2,512]{2,1,0:T(2,128)(2,1)S(1)}, u32[]{:S(2)}, u32[]{:S(2)}) %all-to-all-start.2) | async-done | bytes 65568 | tf_op jit(solution)/shard_map/all_to_all | solution.py:271
  259.3 84.0 %all-reduce.3.cloned.1.call-done = f32[27,64,64]{2,1,0:T(8,128)} async-done(((f32[27,64,64]{2,1,0:T(8,128)}), f32[27,64,64]{2,1,0:T(8,128)}) %all-reduce.3.cloned.1.call-update) | async-done | bytes 442384 | tf_op jit(solution)/shard_map/psum | solution.py:282
  343.3 1.5 multiply_reduce_fusion
  344.7 2.4 fusion.15
  347.1 1.7 copy.82
  349.5 1.9 fusion.16
  (104 shorter events, 8.4 us)
Async XLA Ops:
  8.0 32.9 %copy-start = (f32[3,8,16,128]{3,2,1,0:T(8,128)S(1)}, f32[3,8,16,128]{3,2,1,0:T(8,128)}, u32[]{:S(2)}) copy-start(f32[3,8,16,128]{3,2,1,0:T(8,128)} %param.18) | copy-start | bytes 589828
  8.0 32.9 %copy-start.9 = (bf16[1,54,64]{2,1,0:T(8,128)(2,1)S(1)}, bf16[1,54,64]{2,1,0:T(8,128)(2,1)}, u32[]{:S(2)}) copy-start(bf16[1,54,64]{2,1,0:T(8,128)(2,1)} %param.21) | copy-start | bytes 20740
  8.8 22.3 %collective-permute-start.2 = (f32[3,1,16,128]{3,2,1,0:T(8,128)S(1)}, f32[3,1,16,128]{3,2,1,0:T(8,128)S(1)}, u32[]{:S(2)}, u32[]{:S(2)}) collective-permute-start(f32[3,1,16,128]{3,2,1,0:T(8,128)S(1)} %get-tuple-element.96), channel_id=1, source_target_pairs={{0,32},{32,64},{64,96},{96,128},{128,160},{160,192},{192,224},{224... | collective-permute-start | bytes 73736 | tf_op jit(solution)/shard_map/ppermute | solution.py:33
  10.9 20.3 %collective-permute-start.3 = (f32[3,1,16,128]{3,2,1,0:T(8,128)S(1)}, f32[3,1,16,128]{3,2,1,0:T(8,128)S(1)}, u32[]{:S(2)}, u32[]{:S(2)}) collective-permute-start(f32[3,1,16,128]{3,2,1,0:T(8,128)S(1)} %get-tuple-element.95), channel_id=1, source_target_pairs={{32,0},{64,32},{96,64},{128,96},{160,128},{192,160},{224,192},{0,2... | collective-permute-start | bytes 73736 | tf_op jit(solution)/shard_map/ppermute | solution.py:34
  14.8 49.3 %collective-permute-start = (f32[3,8,1,128]{3,2,1,0:T(1,128)}, f32[3,8,1,128]{3,2,1,0:T(1,128)}, u32[]{:S(2)}, u32[]{:S(2)}) collective-permute-start(f32[3,8,1,128]{3,2,1,0:T(1,128)} %get-tuple-element.94), channel_id=1, source_target_pairs={{0,1},{1,2},{2,3},{3,4},{4,5},{5,6},{6,7},{7,8},{8,9},{9,10},{10,1... | collective-permute-start | bytes 36872 | tf_op jit(solution)/shard_map/ppermute | solution.py:33
  18.8 46.1 %collective-permute-start.1 = (f32[3,8,1,128]{3,2,1,0:T(1,128)S(1)}, f32[3,8,1,128]{3,2,1,0:T(1,128)}, u32[]{:S(2)}, u32[]{:S(2)}) collective-permute-start(f32[3,8,1,128]{3,2,1,0:T(1,128)S(1)} %get-tuple-element.93), channel_id=1, source_target_pairs={{1,0},{2,1},{3,2},{4,3},{5,4},{6,5},{7,6},{8,7},{9,8},{10,9},{11,1... | collective-permute-start | bytes 36872 | tf_op jit(solution)/shard_map/ppermute | solution.py:34
  20.1 10.4 %copy-start.18 = (pred[8]{0:T(512)(128)(4,1)}, pred[8]{0:T(512)(128)(4,1)S(1)}, u32[]{:S(2)}) copy-start(pred[8]{0:T(512)(128)(4,1)S(1)} %compare_and_fusion) | copy-start | bytes 28
  27.7 23.7 %copy-start.16 = (s32[8]{0:T(128)}, s32[8]{0:T(128)S(1)}, u32[]{:S(2)}) copy-start(s32[8]{0:T(128)S(1)} %multiply_add_fusion) | copy-start | bytes 100
  31.2 0.7 copy-start.1
  37.3 8.3 %all-to-all-start = ((bf16[8,2,259]{2,1,0:T(2,128)(2,1)}), bf16[8,2,259]{2,1,0:T(2,128)(2,1)S(1)}, u32[]{:S(2)}, u32[]{:S(2)}) async-start(bf16[8,2,259]{2,1,0:T(2,128)(2,1)} %pad_maximum_fusion.2), calls=%async_computation | async-start | bytes 24576 | tf_op jit(solution)/shard_map/all_to_all | solution.py:50
  40.7 60.5 %all-gather.6.cloned.1.call-start = ((), (), s32[]{:S(2)}) async-start(), calls=%async_computation.4 | async-start | bytes 1179648 | tf_op jit(solution)/shard_map/all_gather | solution.py:64
  45.9 12.5 %copy-start.12 = (f32[16]{0:T(128)}, f32[16]{0:T(128)S(1)}, u32[]{:S(2)}) copy-start(f32[16]{0:T(128)S(1)} %convert_reduce_fusion) | copy-start | bytes 196
  46.0 5.4 %copy-start.7 = (bf16[16,256]{0,1:T(8,128)(2,1)}, bf16[16,256]{0,1:T(8,128)(2,1)S(1)}, u32[]{:S(2)}) copy-start(bf16[16,256]{0,1:T(8,128)(2,1)S(1)} %copy.74) | copy-start | bytes 24580
  52.7 5.0 %copy-start.10 = (bf16[1,2048,2]{1,2,0:T(2,128)(2,1)S(1)}, bf16[1,2048,2]{1,2,0:T(2,128)(2,1)}, u32[]{:S(2)}) copy-start(bf16[1,2048,2]{1,2,0:T(2,128)(2,1)} %param.24) | copy-start | bytes 24580
  53.1 5.6 %copy-start.14 = (bf16[16,2]{0,1:T(2,128)(2,1)}, bf16[16,2]{0,1:T(2,128)(2,1)S(1)}, u32[]{:S(2)}) copy-start(bf16[16,2]{0,1:T(2,128)(2,1)S(1)} %copy.88) | copy-start | bytes 196
  53.1 12.7 %copy-start.2 = (f32[3,8,16,128]{3,2,1,0:T(8,128)S(1)}, f32[3,8,16,128]{3,2,1,0:T(8,128)}, u32[]{:S(2)}) copy-start(f32[3,8,16,128]{3,2,1,0:T(8,128)} %copy-done.1) | copy-start | bytes 589828
  57.7 0.6 copy-start.5
  64.1 279.2 %all-reduce.3.cloned.1.call-start = ((), (), s32[]{:S(2)}) async-start(), calls=%async_computation.3 | async-start | bytes 1769472 | tf_op jit(solution)/shard_map/psum | solution.py:282
  66.6 6.1 %copy-start.3 = (f32[16,4,4,8,64]{4,0,3,2,1:T(8,128)S(1)}, f32[16,4,4,8,64]{4,0,3,2,1:T(8,128)}, u32[]{:S(2)}) copy-start(f32[16,4,4,8,64]{4,0,3,2,1:T(8,128)} %get-tuple-element.98) | copy-start | bytes 1572868
  72.7 4.4 %copy-start.4 = (bf16[1,27,64,64]{3,2,1,0:T(8,128)(2,1)S(1)}, bf16[1,27,64,64]{3,2,1,0:T(8,128)(2,1)}, u32[]{:S(2)}) copy-start(bf16[1,27,64,64]{3,2,1,0:T(8,128)(2,1)} %param.22) | copy-start | bytes 663556
  72.7 4.4 %copy-start.8 = (bf16[16,256]{0,1:T(8,128)(2,1)S(1)}, bf16[16,256]{0,1:T(8,128)(2,1)}, u32[]{:S(2)}) copy-start(bf16[16,256]{0,1:T(8,128)(2,1)} %copy-done.7) | copy-start | bytes 24580
  76.8 24.4 %copy-start.6 = (bf16[16,2048]{1,0:T(8,128)(2,1)S(1)}, bf16[16,2048]{1,0:T(8,128)(2,1)}, u32[]{:S(2)}) copy-start(bf16[16,2048]{1,0:T(8,128)(2,1)} %copy-done.5) | copy-start | bytes 196612
  76.8 24.4 %copy-start.13 = (f32[16]{0:T(128)S(1)}, f32[16]{0:T(128)}, u32[]{:S(2)}) copy-start(f32[16]{0:T(128)} %copy-done.12) | copy-start | bytes 196
  76.8 24.4 %copy-start.15 = (bf16[16,2]{0,1:T(2,128)(2,1)S(1)}, bf16[16,2]{0,1:T(2,128)(2,1)}, u32[]{:S(2)}) copy-start(bf16[16,2]{0,1:T(2,128)(2,1)} %copy-done.14) | copy-start | bytes 196
  76.8 160.9 %copy-start.11 = (bf16[1,2048,2]{1,2,0:T(2,128)(2,1)S(1)}, bf16[1,2048,2]{1,2,0:T(2,128)(2,1)}, u32[]{:S(2)}) copy-start(bf16[1,2048,2]{1,2,0:T(2,128)(2,1)} %param.24) | copy-start | bytes 24580
  76.8 172.6 %copy-start.17 = (s32[8]{0:T(128)S(1)}, s32[8]{0:T(128)}, u32[]{:S(2)}) copy-start(s32[8]{0:T(128)} %copy-done.16) | copy-start | bytes 100
  76.8 270.3 %all-gather.8.cloned.1.call-start = ((), (), s32[]{:S(2)}) async-start(), calls=%async_computation.5 | async-start | bytes 3145728 | tf_op jit(solution)/shard_map/all_gather | solution.py:64
  102.0 137.1 %all-to-all-start.1 = ((f32[8,2,2]{1,2,0:T(2,128)}), f32[8,2,2]{1,2,0:T(2,128)S(1)}, u32[]{:S(2)}, u32[]{:S(2)}) async-start(f32[8,2,2]{1,2,0:T(2,128)} %copy.77), calls=%async_computation.1 | async-start | bytes 16384 | tf_op jit(solution)/shard_map/all_to_all | solution.py:266
  239.1 20.0 %all-to-all-start.2 = ((bf16[32,2,512]{2,1,0:T(2,128)(2,1)}), bf16[32,2,512]{2,1,0:T(2,128)(2,1)S(1)}, u32[]{:S(2)}, u32[]{:S(2)}) async-start(bf16[32,2,512]{2,1,0:T(2,128)(2,1)} %reshape.333), calls=%async_computation.2 | async-start | bytes 131072 | tf_op jit(solution)/shard_map/all_to_all | solution.py:271
Sparse Core Ops, SparseCore 0:
  64.2 36.9 all-gather.5
  103.1 19.9 all-gather.7
Sparse Core Ops, SparseCore 1:
  76.8 266.4 all-reduce.2
where the time goes:
time: 360 us; the launch traced here: 359 us
  blocking collectives  134 us (37%)
  waiting for transfers between devices  117 us (32%)
  matrix products  31 us (9%)
  starting transfers between devices  27.4 us (8%)
  between operations  16.8 us (5%)
  other arithmetic  16.6 us (5%)
  local copies, waits for them, and re-layouts  15.5 us (4%)
    psum x1, blocking collectives, body(): lax.psum((grad_one, grad_two, grad_out), STREAM)  129 us
    psum x1, waiting for transfers between devices, body(): lax.psum((grad_one, grad_two, grad_out), STREAM)  84 us
    all_gather x2, waiting for transfers between devices, gather_in_order(): tiles = lax.all_gather(tiles, axes[k])  19.8 us
    all_to_all x1, starting transfers between devices, body(): lax.all_to_all(features, STREAM, split_axis=1, concat_axis=0, tiled=True)  10.2 us
    all_to_all x1, waiting for transfers between devices, body(): lax.all_to_all(features, STREAM, split_axis=1, concat_axis=0, tiled=True)  8.98 us
    transpose x2, matrix products, conv_filter(): return jnp.moveaxis(taps, 0, 3)  7.83 us
  transfers between devices with their start and end apart: 10, of which 4 were waited for; matrix products, arithmetic and copies ran while one was open for 16% of the time, Pallas kernels for 0%

commit v1 on v0

--- a/solution.py
+++ b/solution.py
@@ -279,7 +279,9 @@
     )
     own_rows = lax.dynamic_slice_in_dim(w_hidden[0], flow_place * share_rows, share_rows, 0)
     new_w_hidden = row_update(own_rows, grad_hidden)[None]
-    grad_one, grad_two, grad_out = lax.psum((grad_one, grad_two, grad_out), STREAM)
+    grad_one, grad_two, grad_out = lax.psum(
+        lax.psum((grad_one, grad_two, grad_out), ("stream_1", "stream_2")), "stream_0"
+    )
     new_k_second = row_update(k_second[0], grad_two)
     new_k_first = row_update(k_first[0], grad_one)
     new_w_out = whole_update(w_out[0], grad_out)

time: 360 us -> 213 us (0.59)
  blocking collectives: 134 us -> 42.9 us
  waiting for transfers between devices: 117 us -> 58.6 us
  starting transfers between devices: 27.4 us -> 32.9 us
    psum x1 -> x2, blocking collectives: 129 us -> 37.5 us  [the longest x1 23.9 us: body(): lax.psum(lax.psum((grad_one, grad_two, grad_out), ('stream_1', 'stream_2'...]
    psum x1 -> x2, waiting for transfers between devices: 84 us -> 31.5 us  [the longest x1 31.4 us: body(): lax.psum((grad_one, grad_two, grad_out), ('stream_1', 'stream_2'))]
    all_gather x2, waiting for transfers between devices: 19.8 us -> 11.7 us  [gather_in_order(): tiles = lax.all_gather(tiles, axes[k])]
    all_to_all x1, starting transfers between devices: 10.2 us -> 14.2 us  [body(): lax.all_to_all(features, STREAM, split_axis=1, concat_axis=0, tiled=True)]
  transfers between devices with their start and end apart: 10 -> 11, of which waited for: 4 -> 5; matrix products, arithmetic and copies ran while one was open for 16% -> 15% of each run, Pallas kernels for 0% -> 0%
where the time goes in v1:
time: 213 us; the launch traced here: 212 us
  waiting for transfers between devices  58.6 us (28%)
  blocking collectives  42.9 us (20%)
  starting transfers between devices  32.9 us (15%)
  matrix products  28.1 us (13%)
  other arithmetic  17.4 us (8%)
  between operations  17 us (8%)
  local copies, waits for them, and re-layouts  15.5 us (7%)
    psum x1, waiting for transfers between devices, body(): lax.psum((grad_one, grad_two, grad_out), ('stream_1', 'stream_2'))  31.4 us
    psum x1, blocking collectives, body(): lax.psum(lax.psum((grad_one, grad_two, grad_out), ('stream_1', 'stream_2'...  23.9 us
    all_to_all x1, starting transfers between devices, body(): lax.all_to_all(features, STREAM, split_axis=1, concat_axis=0, tiled=True)  14.2 us
    psum x1, blocking collectives, body(): lax.psum((grad_one, grad_two, grad_out), ('stream_1', 'stream_2'))  13.6 us
    all_gather x2, waiting for transfers between devices, gather_in_order(): tiles = lax.all_gather(tiles, axes[k])  11.7 us
    all_to_all x1, waiting for transfers between devices, body(): lax.all_to_all(features, STREAM, split_axis=1, concat_axis=0, tiled=True)  9.19 us
    transpose x2, matrix products, conv_filter(): return jnp.moveaxis(taps, 0, 3)  8.93 us
    ppermute x2, starting transfers between devices, extended(): lax.ppermute(last, axis, up)  8.42 us
  transfers between devices with their start and end apart: 11, of which 5 were waited for; matrix products, arithmetic and copies ran while one was open for 15% of the time, Pallas kernels for 0%

profile of v1, /device:TPU:1, one launch (start us, length us, event | category | flops | bytes accessed | tf_op | source)
XLA Modules:
  0.0 212.4 jit_solution(17892379009188051974)
XLA Ops:
  8.0 0.8 fusion.47
  8.8 2.0 collective-permute-start.2
  10.9 2.3 %collective-permute-start.3 = (f32[3,1,16,128]{3,2,1,0:T(8,128)S(1)}, f32[3,1,16,128]{3,2,1,0:T(8,128)S(1)}, u32[]{:S(2)}, u32[]{:S(2)}) collective-permute-start(f32[3,1,16,128]{3,2,1,0:T(8,128)S(1)} %get-tuple-element.97), channel_id=1, source_target_pairs={{32,0},{64,32},{96,64},{128,96},{160,128},{192,160},{224,192},{0,2... | collective-permute-start | bytes 73736 | tf_op jit(solution)/shard_map/ppermute | solution.py:34
  13.2 0.7 fusion.41
  13.9 0.7 compare_and_fusion
  14.5 0.9 fusion.44
  15.4 1.5 fusion.23
  16.9 0.7 fusion.34
  17.7 0.8 select_reduce_fusion
  18.5 0.7 multiply_add_fusion
  19.2 1.2 reshape.297
  22.7 1.1 reshape.300
  25.1 0.7 pad_maximum_fusion.2
  25.8 3.3 %all-to-all-start = ((bf16[8,2,259]{2,1,0:T(2,128)(2,1)}), bf16[8,2,259]{2,1,0:T(2,128)(2,1)S(1)}, u32[]{:S(2)}, u32[]{:S(2)}) async-start(bf16[8,2,259]{2,1,0:T(2,128)(2,1)} %pad_maximum_fusion.2), calls=%async_computation | async-start | bytes 24576 | tf_op jit(solution)/shard_map/all_to_all | solution.py:50
  29.4 4.7 %all-to-all-done = bf16[8,2,259]{2,1,0:T(2,128)(2,1)S(1)} async-done(((bf16[8,2,259]{2,1,0:T(2,128)(2,1)}), bf16[8,2,259]{2,1,0:T(2,128)(2,1)S(1)}, u32[]{:S(2)}, u32[]{:S(2)}) %all-to-all-start) | async-done | bytes 8320 | tf_op jit(solution)/shard_map/all_to_all | solution.py:50
  34.8 0.7 convert_reduce_fusion
  35.6 0.9 convolution_multiply_fusion.4
  36.6 3.1 %fusion.14 = (f32[16,4,4,8,64]{4,0,3,2,1:T(8,128)S(1)}, f32[16,4,4,8,64]{4,0,3,2,1:T(8,128)}) fusion(bf16[3,3,3,64,64]{4,3,2,1,0:T(8,128)(2,1)S(1)} %bitcast.139, f32[16,4,4,8,64]{4,0,3,2,1:T(8,128)S(1)} %convolution_multiply_fusion.4), kind=kOutput, calls=%fused_computation.26 | convolution fusion | flops 289669120 | bytes 1794048 | tf_op jit(solution)/shard_map/conv_general_dilated | solution.py:130
  40.1 4.6 %multiply_convert_fusion.3 = (bf16[16,2048]{1,0:T(8,128)(2,1)S(1)}, f32[16,2048]{1,0:T(8,128)S(1)}) fusion(bf16[16,2048]{1,0:T(8,128)(2,1)S(1)} %convert_element_type.116, bf16[1,2048,2048]{2,1,0:T(8,128)(2,1)} %param.23), kind=kOutput, calls=%fused_computation.50 | convolution fusion | flops 134414336 | bytes 8650752 | tf_op jit(solution)/shard_map/dot_general | solution.py:164
  45.7 5.7 %fusion.8 = f32[16,2048]{1,0:T(8,128)S(1)} fusion(bf16[16,2048]{1,0:T(8,128)(2,1)S(1)} %fusion.11, bf16[1,2048,2048]{2,1,0:T(8,128)(2,1)} %param.23), kind=kOutput, calls=%fused_computation.9 | convolution fusion | flops 134250496 | bytes 8585216 | tf_op jit(solution)/shard_map/dot_general | solution.py:174
  52.2 3.6 %convolution_multiply_fusion.5 = f32[3,3,3,64,64]{4,3,2,1,0:T(8,128)} fusion(bf16[16,4,4,8,64]{4,0,3,2,1:T(8,128)(2,1)S(1)} %multiply_convert_fusion, f32[16,4,4,8,64]{4,0,3,2,1:T(8,128)S(1)} %convolution_multiply_fusion.4), kind=kOutput, calls=%fused_computation.16 | convolution fusion | flops 289124352 | bytes 1228800 | tf_op jit(solution)/shard_map/transpose | solution.py:144
  55.9 5.4 %all-gather = bf16[32,2048]{1,0:T(8,128)(2,1)} all-gather(bf16[16,2048]{1,0:T(8,128)(2,1)S(1)} %copy-done.5), channel_id=2, replica_groups=mesh['wall'=8,'stream_0'=8,'stream_1'=2,'stream_2'=2] {'stream_1'}, dimensions={0}, use_global_device_ids=true | all-gather | bytes 196608 | tf_op jit(solution)/shard_map/all_gather | solution.py:64
  61.4 0.6 fusion.46
  62.0 6.4 %collective-permute-start = (f32[3,8,1,128]{3,2,1,0:T(1,128)}, f32[3,8,1,128]{3,2,1,0:T(1,128)}, u32[]{:S(2)}, u32[]{:S(2)}) collective-permute-start(f32[3,8,1,128]{3,2,1,0:T(1,128)} %get-tuple-element.96), channel_id=1, source_target_pairs={{0,1},{1,2},{2,3},{3,4},{4,5},{5,6},{6,7},{7,8},{8,9},{9,10},{10,1... | collective-permute-start | bytes 36872 | tf_op jit(solution)/shard_map/ppermute | solution.py:33
  69.4 0.6 slice_bitcast_fusion.2
  70.1 1.3 slice_add_fusion.5
  71.4 0.8 scatter-add.14
  72.2 1.5 collective-permute-done.1
  73.6 1.3 slice_add_fusion.4
  75.0 0.8 scatter-add.15
  75.7 1.7 fusion.20
  77.4 31.4 %all-reduce.5.cloned.1.call-done = f32[27,64,64]{2,1,0:T(8,128)} async-done(((f32[27,64,64]{2,1,0:T(8,128)}), f32[27,64,64]{2,1,0:T(8,128)}) %all-reduce.5.cloned.1.call-update) | async-done | bytes 442384 | tf_op jit(solution)/shard_map/psum | solution.py:283
  108.9 5.3 %convolution_multiply_fusion.6 = f32[3,3,3,2,64]{4,3,2,1,0:T(2,128)S(1)} fusion(bf16[16,2,4,4,8]{0,4,3,2,1:T(8,128)(2,1)} %bitcast.141, bf16[16,4,4,8,64]{4,0,3,2,1:T(8,128)(2,1)S(1)} %multiply_convert_fusion, bf16[3,3,3,64,64]{4,3,2,1,0:T(8,128)(2,1)} %bitcast.138, f32[16,4,4,8,64]{4,0,3,2,1:T(8,128)S(1)} %convolution_multiply_fusion.4), kind=kOutput, calls=%fused_computation.20 | convolution fusion | flops 298683776 | bytes 1029632 | tf_op jit(solution)/shard_map/transpose | solution.py:144
  115.2 4.2 %all-to-all-start.1 = ((f32[8,2,2]{1,2,0:T(2,128)}), f32[8,2,2]{1,2,0:T(2,128)S(1)}, u32[]{:S(2)}, u32[]{:S(2)}) async-start(f32[8,2,2]{1,2,0:T(2,128)} %copy.77), calls=%async_computation.1 | async-start | bytes 16384 | tf_op jit(solution)/shard_map/all_to_all | solution.py:266
  119.4 13.6 %all-reduce.1 = (f32[54,64]{1,0:T(8,128)S(1)}, f32[2048,2]{0,1:T(2,128)S(1)}) all-reduce(f32[54,64]{1,0:T(8,128)S(1)} %reshape.304, f32[2048,2]{0,1:T(2,128)S(1)} %convolution_multiply_fusion.1), channel_id=1, replica_groups=mesh['wall'=8,'stream_0'=8,'stream_1'=2,'stream_2'=2] {'stream_1','strea..., use_global_device_ids=true, to_apply=%region_5.6 | all-reduce | flops 7552 | bytes 60416 | tf_op jit(solution)/shard_map/psum | solution.py:283
  133.0 23.9 %all-reduce = (f32[54,64]{1,0:T(8,128)S(1)}, f32[2048,2]{0,1:T(2,128)S(1)}) all-reduce(f32[54,64]{1,0:T(8,128)S(1)} %get-tuple-element.86, f32[2048,2]{0,1:T(2,128)S(1)} %get-tuple-element.87), channel_id=1, replica_groups=mesh['wall'=8,'stream_0'=8,'stream_1'=2,'stream_2'=2] {'stream_0'}, use_global_device_ids=true, to_apply=%region_6.7 | all-reduce | flops 7552 | bytes 60416 | tf_op jit(solution)/shard_map/psum | solution.py:282
  157.2 0.6 broadcast_in_dim.48
  157.8 0.6 multiply_reduce_fusion.3
  159.1 0.6 fusion.29
  159.7 0.8 reshape.333
  160.5 14.2 %all-to-all-start.2 = ((bf16[32,2,512]{2,1,0:T(2,128)(2,1)}), bf16[32,2,512]{2,1,0:T(2,128)(2,1)S(1)}, u32[]{:S(2)}, u32[]{:S(2)}) async-start(bf16[32,2,512]{2,1,0:T(2,128)(2,1)} %reshape.333), calls=%async_computation.2 | async-start | bytes 131072 | tf_op jit(solution)/shard_map/all_to_all | solution.py:271
  174.8 0.8 fusion.33
  175.6 9.2 %all-to-all-done.2 = bf16[32,2,512]{2,1,0:T(2,128)(2,1)S(1)} async-done(((bf16[32,2,512]{2,1,0:T(2,128)(2,1)}), bf16[32,2,512]{2,1,0:T(2,128)(2,1)S(1)}, u32[]{:S(2)}, u32[]{:S(2)}) %all-to-all-start.2) | async-done | bytes 65568 | tf_op jit(solution)/shard_map/all_to_all | solution.py:271
  185.0 1.5 multiply_reduce_fusion
  186.5 2.4 %fusion.15 = f32[1,27,64,64]{3,2,1,0:T(8,128)} fusion(f32[27,64,64]{2,1,0:T(8,128)} %all-reduce.7.cloned.1.call-done, bf16[1,27,64,64]{3,2,1,0:T(8,128)(2,1)S(1)} %copy-done.3, f32[27,64]{1,0:T(8,128)S(1)} %add_sqrt_fusion), kind=kLoop, calls=%fused_computation.30 | loop fusion | flops 442368 | bytes 1112832 | tf_op jit(solution)/shard_map/broadcast_in_dim | solution.py:288
  188.8 11.7 %all-gather.8.cloned.1.call-done = bf16[16,2,16,2048]{3,2,1,0:T(8,128)(2,1)} async-done(((bf16[8,2,16,2048]{3,2,1,0:T(8,128)(2,1)}), bf16[16,2,16,2048]{3,2,1,0:T(8,128)(2,1)}) %all-gather.8.cloned.1.call-update) | async-done | bytes 2097168 | tf_op jit(solution)/shard_map/all_gather | solution.py:64
  200.5 1.7 copy.82
  202.9 1.9 fusion.16
  (116 shorter events, 9.9 us)
Async XLA Ops:
  8.0 21.4 %copy-start.10 = (bf16[1,54,64]{2,1,0:T(8,128)(2,1)S(1)}, bf16[1,54,64]{2,1,0:T(8,128)(2,1)}, u32[]{:S(2)}) copy-start(bf16[1,54,64]{2,1,0:T(8,128)(2,1)} %param.21) | copy-start | bytes 20740
  8.0 28.5 %copy-start.2 = (bf16[1,27,64,64]{3,2,1,0:T(8,128)(2,1)S(1)}, bf16[1,27,64,64]{3,2,1,0:T(8,128)(2,1)}, u32[]{:S(2)}) copy-start(bf16[1,27,64,64]{3,2,1,0:T(8,128)(2,1)} %param.22) | copy-start | bytes 663556
  8.8 13.8 %collective-permute-start.2 = (f32[3,1,16,128]{3,2,1,0:T(8,128)S(1)}, f32[3,1,16,128]{3,2,1,0:T(8,128)S(1)}, u32[]{:S(2)}, u32[]{:S(2)}) collective-permute-start(f32[3,1,16,128]{3,2,1,0:T(8,128)S(1)} %get-tuple-element.98), channel_id=1, source_target_pairs={{0,32},{32,64},{64,96},{96,128},{128,160},{160,192},{192,224},{224... | collective-permute-start | bytes 73736 | tf_op jit(solution)/shard_map/ppermute | solution.py:33
  10.9 11.8 %collective-permute-start.3 = (f32[3,1,16,128]{3,2,1,0:T(8,128)S(1)}, f32[3,1,16,128]{3,2,1,0:T(8,128)S(1)}, u32[]{:S(2)}, u32[]{:S(2)}) collective-permute-start(f32[3,1,16,128]{3,2,1,0:T(8,128)S(1)} %get-tuple-element.97), channel_id=1, source_target_pairs={{32,0},{64,32},{96,64},{128,96},{160,128},{192,160},{224,192},{0,2... | collective-permute-start | bytes 73736 | tf_op jit(solution)/shard_map/ppermute | solution.py:34
  19.2 17.4 %copy-start.21 = (s32[8]{0:T(128)}, s32[8]{0:T(128)S(1)}, u32[]{:S(2)}) copy-start(s32[8]{0:T(128)S(1)} %multiply_add_fusion) | copy-start | bytes 100
  25.8 8.3 %all-to-all-start = ((bf16[8,2,259]{2,1,0:T(2,128)(2,1)}), bf16[8,2,259]{2,1,0:T(2,128)(2,1)S(1)}, u32[]{:S(2)}, u32[]{:S(2)}) async-start(bf16[8,2,259]{2,1,0:T(2,128)(2,1)} %pad_maximum_fusion.2), calls=%async_computation | async-start | bytes 24576 | tf_op jit(solution)/shard_map/all_to_all | solution.py:50
  29.2 79.6 %all-reduce.5.cloned.1.call-start = ((), (), s32[]{:S(2)}) async-start(), calls=%async_computation.3 | async-start | bytes 1769472 | tf_op jit(solution)/shard_map/psum | solution.py:283
  35.6 4.0 %copy-start.8 = (bf16[16,256]{0,1:T(8,128)(2,1)}, bf16[16,256]{0,1:T(8,128)(2,1)S(1)}, u32[]{:S(2)}) copy-start(bf16[16,256]{0,1:T(8,128)(2,1)S(1)} %copy.74) | copy-start | bytes 24580
  36.5 3.5 %copy-start.11 = (bf16[16,2]{1,0:T(8,128)(2,1)S(1)}, bf16[16,2]{1,0:T(8,128)(2,1)}, u32[]{:S(2)}) copy-start(bf16[16,2]{1,0:T(8,128)(2,1)} %split.14) | copy-start | bytes 196
  39.8 5.0 %copy-start.13 = (bf16[1,2048,2]{1,2,0:T(2,128)(2,1)S(1)}, bf16[1,2048,2]{1,2,0:T(2,128)(2,1)}, u32[]{:S(2)}) copy-start(bf16[1,2048,2]{1,2,0:T(2,128)(2,1)} %param.24) | copy-start | bytes 24580
  39.8 5.6 %copy-start.17 = (f32[16]{0:T(128)S(1)}, f32[16]{0:T(128)}, u32[]{:S(2)}) copy-start(f32[16]{0:T(128)} %convert_reduce_fusion) | copy-start | bytes 196
  40.1 5.5 %copy-start.19 = (bf16[16,2]{0,1:T(2,128)(2,1)}, bf16[16,2]{0,1:T(2,128)(2,1)S(1)}, u32[]{:S(2)}) copy-start(bf16[16,2]{0,1:T(2,128)(2,1)S(1)} %copy.88) | copy-start | bytes 196
  44.7 0.6 copy-start.6
  44.8 7.0 %copy-start.1 = (f32[16,4,4,8,64]{4,0,3,2,1:T(8,128)S(1)}, f32[16,4,4,8,64]{4,0,3,2,1:T(8,128)}, u32[]{:S(2)}) copy-start(f32[16,4,4,8,64]{4,0,3,2,1:T(8,128)} %get-tuple-element.100) | copy-start | bytes 1572868
  44.9 6.8 %copy-start.15 = (f32[16,2]{0,1:T(2,128)}, f32[16,2]{0,1:T(2,128)S(1)}, u32[]{:S(2)}) copy-start(f32[16,2]{0,1:T(2,128)S(1)} %convolution_multiply_fusion.7) | copy-start | bytes 388
  45.6 6.1 %copy-start.4 = (bf16[16,2048]{1,0:T(8,128)(2,1)}, bf16[16,2048]{1,0:T(8,128)(2,1)S(1)}, u32[]{:S(2)}) copy-start(bf16[16,2048]{1,0:T(8,128)(2,1)S(1)} %fusion.11) | copy-start | bytes 196612
  51.7 9.6 %copy-start = (f32[3,8,16,128]{3,2,1,0:T(8,128)S(1)}, f32[3,8,16,128]{3,2,1,0:T(8,128)}, u32[]{:S(2)}) copy-start(f32[3,8,16,128]{3,2,1,0:T(8,128)} %param.18) | copy-start | bytes 589828
  52.2 3.7 %copy-start.5 = (bf16[16,2048]{1,0:T(8,128)(2,1)S(1)}, bf16[16,2048]{1,0:T(8,128)(2,1)}, u32[]{:S(2)}) copy-start(bf16[16,2048]{1,0:T(8,128)(2,1)} %copy-done.4) | copy-start | bytes 196612
  52.2 16.2 %copy-start.12 = (f32[32,16,1,1]{0,1,3,2:T(8,128)S(1)}, f32[32,16,1,1]{0,1,3,2:T(8,128)}, u32[]{:S(2)}) copy-start(f32[32,16,1,1]{0,1,3,2:T(8,128)} %constant.248) | copy-start | bytes 6148
  52.2 16.7 %copy-start.9 = (f32[256,128,1,1]{1,0,3,2:T(8,128)S(1)}, f32[256,128,1,1]{1,0,3,2:T(8,128)}, u32[]{:S(2)}) copy-start(f32[256,128,1,1]{1,0,3,2:T(8,128)} %constant.250) | copy-start | bytes 393220
  55.8 58.5 %all-gather.6.cloned.1.call-start = ((), (), s32[]{:S(2)}) async-start(), calls=%async_computation.5 | async-start | bytes 1179648 | tf_op jit(solution)/shard_map/all_gather | solution.py:64
  61.3 123.6 %all-reduce.7.cloned.1.call-start = ((), (), s32[]{:S(2)}) async-start(), calls=%async_computation.4 | async-start | bytes 1769472 | tf_op jit(solution)/shard_map/psum | solution.py:282
  62.0 8.1 %collective-permute-start = (f32[3,8,1,128]{3,2,1,0:T(1,128)}, f32[3,8,1,128]{3,2,1,0:T(1,128)}, u32[]{:S(2)}, u32[]{:S(2)}) collective-permute-start(f32[3,8,1,128]{3,2,1,0:T(1,128)} %get-tuple-element.96), channel_id=1, source_target_pairs={{0,1},{1,2},{2,3},{3,4},{4,5},{5,6},{6,7},{7,8},{8,9},{9,10},{10,1... | collective-permute-start | bytes 36872 | tf_op jit(solution)/shard_map/ppermute | solution.py:33
  68.4 5.2 %collective-permute-start.1 = (f32[3,8,1,128]{3,2,1,0:T(1,128)}, f32[3,8,1,128]{3,2,1,0:T(1,128)}, u32[]{:S(2)}, u32[]{:S(2)}) collective-permute-start(f32[3,8,1,128]{3,2,1,0:T(1,128)} %get-tuple-element.95), channel_id=1, source_target_pairs={{1,0},{2,1},{3,2},{4,3},{5,4},{6,5},{7,6},{8,7},{9,8},{10,9},{11,1... | collective-permute-start | bytes 36872 | tf_op jit(solution)/shard_map/ppermute | solution.py:34
  108.8 5.5 %copy-start.7 = (bf16[16,2048]{1,0:T(8,128)(2,1)S(1)}, bf16[16,2048]{1,0:T(8,128)(2,1)}, u32[]{:S(2)}) copy-start(bf16[16,2048]{1,0:T(8,128)(2,1)} %copy-done.6) | copy-start | bytes 196612
  108.8 5.5 %copy-start.16 = (f32[16,2]{0,1:T(2,128)S(1)}, f32[16,2]{0,1:T(2,128)}, u32[]{:S(2)}) copy-start(f32[16,2]{0,1:T(2,128)} %copy-done.15) | copy-start | bytes 388
  108.8 5.5 %copy-start.18 = (f32[16]{0:T(128)S(1)}, f32[16]{0:T(128)}, u32[]{:S(2)}) copy-start(f32[16]{0:T(128)} %convert_reduce_fusion) | copy-start | bytes 196
  108.9 5.5 %copy-start.20 = (bf16[16,2]{0,1:T(2,128)(2,1)S(1)}, bf16[16,2]{0,1:T(2,128)(2,1)}, u32[]{:S(2)}) copy-start(bf16[16,2]{0,1:T(2,128)(2,1)} %copy-done.19) | copy-start | bytes 196
  108.9 50.3 %copy-start.14 = (bf16[1,2048,2]{1,2,0:T(2,128)(2,1)S(1)}, bf16[1,2048,2]{1,2,0:T(2,128)(2,1)}, u32[]{:S(2)}) copy-start(bf16[1,2048,2]{1,2,0:T(2,128)(2,1)} %param.24) | copy-start | bytes 24580
  108.9 66.0 %copy-start.22 = (s32[8]{0:T(128)S(1)}, s32[8]{0:T(128)}, u32[]{:S(2)}) copy-start(s32[8]{0:T(128)} %copy-done.21) | copy-start | bytes 100
  108.9 77.6 %copy-start.3 = (bf16[1,27,64,64]{3,2,1,0:T(8,128)(2,1)S(1)}, bf16[1,27,64,64]{3,2,1,0:T(8,128)(2,1)}, u32[]{:S(2)}) copy-start(bf16[1,27,64,64]{3,2,1,0:T(8,128)(2,1)} %param.22) | copy-start | bytes 663556
  108.9 91.6 %all-gather.8.cloned.1.call-start = ((), (), s32[]{:S(2)}) async-start(), calls=%async_computation.6 | async-start | bytes 3145728 | tf_op jit(solution)/shard_map/all_gather | solution.py:64
  115.2 45.3 %all-to-all-start.1 = ((f32[8,2,2]{1,2,0:T(2,128)}), f32[8,2,2]{1,2,0:T(2,128)S(1)}, u32[]{:S(2)}, u32[]{:S(2)}) async-start(f32[8,2,2]{1,2,0:T(2,128)} %copy.77), calls=%async_computation.1 | async-start | bytes 16384 | tf_op jit(solution)/shard_map/all_to_all | solution.py:266
  160.5 24.3 %all-to-all-start.2 = ((bf16[32,2,512]{2,1,0:T(2,128)(2,1)}), bf16[32,2,512]{2,1,0:T(2,128)(2,1)S(1)}, u32[]{:S(2)}, u32[]{:S(2)}) async-start(bf16[32,2,512]{2,1,0:T(2,128)(2,1)} %reshape.333), calls=%async_computation.2 | async-start | bytes 131072 | tf_op jit(solution)/shard_map/all_to_all | solution.py:271
Sparse Core Ops, SparseCore 0:
  56.0 52.7 all-reduce.4
Sparse Core Ops, SparseCore 1:
  61.4 38.4 all-gather.5
  108.9 70.1 all-reduce.6
  180.8 19.7 all-gather.7
